TPU v7x, 256 devices: a whole 4x4x8 slice. The times are simulated.
256 devices in a mesh: act: 32 (over x, y, core), pix: 8 (over z).
Axes of the slice: x: 4, y: 4, z: 8, core: 2. Of those that a mesh axis runs over, the one named last changes fastest.
Arguments:
- pixel_index: int32 [8, 512], P('pix'), may hold values from 0 to 65535
- act_map: int32 [32768], P('act'), may hold values from 0 to 32767, each once
- omega: bfloat16 [32768, 128], P('act'), may hold values from -6 to 6
- pupil_field: float32 [8, 2, 32768], P('pix', None, 'act'), may hold values from -6 to 6
- channel_scale: float32 [8], P('pix'), may hold values from 0.9 to 1.1
- channel_flux: float32 [8], P('pix'), may hold values from 0.3 to 3
Outputs:
- basis_out: float32 [8, 1024, 128], P('pix', 'act')
- projection: float32 [128, 32768], P('pix', 'act')
- r_factor: float32 [128, 128], replicated
Inputs may be any that keep to these rules, and one draw needn't show every extreme that they name: `act_map`: every number of 0 to 32767 appears once. `pixel_index`: pixels of a channel may repeat.
All inputs are finite; a program needn't handle non-finite values.
Results may differ from a plain program's by a relative error of at most 0.0048.
Values may be sent and summed in bfloat16 or wider, within the bound.
No kernel may reach another device: no remote copies, remote signals or barrier semaphores. Data moves between devices by JAX's collectives and lax.ppermute only.
A program may use at most 64 MiB of HBM per device.

v0:
```python
import math
import jax
import jax.numpy as jnp
from jax import lax
from jax.sharding import PartitionSpec as P

GRID = 128
FOCAL = 256
RANK = 128
ACT = 32768
TWO_PI = 2.0 * math.pi
INFL_RATE = 4.5
DEFOCUS_RATE = 6.0


def jacobian_planes(pixels, wave_scale, flux_level, codes, field_re, field_im):
    delta_u = pixels // FOCAL - FOCAL // 2
    delta_v = pixels % FOCAL - FOCAL // 2
    mirror = codes // (GRID * GRID)
    column_x = codes // GRID % GRID - GRID // 2
    column_y = codes % GRID - GRID // 2
    phase_int = delta_u[:, None] * column_x[None, :] + delta_v[:, None] * column_y[None, :]
    radius = (delta_u * delta_u + delta_v * delta_v).astype(jnp.float32)
    amplitude = flux_level * jnp.exp(-INFL_RATE * radius / (FOCAL * FOCAL))
    defocus = radius * (TWO_PI * DEFOCUS_RATE / (FOCAL * FOCAL)) / wave_scale
    phase_angle = mirror.astype(jnp.float32)[None, :] * defocus[
        :, None
    ] - TWO_PI / FOCAL * wave_scale * phase_int.astype(jnp.float32)
    cosine = jnp.cos(phase_angle)
    sine_part = jnp.sin(phase_angle)
    real_part = amplitude[:, None] * (field_re[None, :] * cosine - field_im[None, :] * sine_part)
    imag_part = amplitude[:, None] * (field_re[None, :] * sine_part + field_im[None, :] * cosine)
    return (real_part.astype(jnp.bfloat16), imag_part.astype(jnp.bfloat16))


def gram_of(sketch):
    return lax.dot_general(
        sketch,
        sketch,
        (((0,), (0,)), ((), ())),
        precision=lax.Precision.HIGHEST,
        preferred_element_type=jnp.float32,
    )


def on_device(pixel_index, act_map, omega, pupil_field, channel_scale, channel_flux):
    pixels = pixel_index[0]
    npix = pixels.shape[0]
    rows_dev = 2 * npix
    act_count = lax.axis_size("act")
    pix_count = lax.axis_size("pix")
    total_rows = rows_dev * pix_count
    share_pix = npix // act_count
    real_rows, imag_rows = jacobian_planes(
        pixels, channel_scale[0], channel_flux[0], act_map, pupil_field[0, 0], pupil_field[0, 1]
    )
    jac = jnp.concatenate([real_rows, imag_rows], axis=0)
    partial_sketch = jnp.dot(jac, omega, preferred_element_type=jnp.float32)
    sketch = lax.psum(partial_sketch, "act")
    gram_matrix = lax.psum(gram_of(sketch), "pix")
    lower_factor = jnp.linalg.cholesky(gram_matrix)
    basis = jax.scipy.linalg.solve_triangular(lower_factor, sketch.T, lower=True).T
    first = lax.axis_index("act") * share_pix
    own_re = lax.dynamic_slice_in_dim(basis, first, share_pix, 0)
    own_im = lax.dynamic_slice_in_dim(basis, npix + first, share_pix, 0)
    own_basis = jnp.stack([own_re, own_im], axis=1).reshape(2 * share_pix, RANK)
    coarse = basis.astype(jnp.bfloat16)
    partial_value = lax.dot_general(
        coarse, jac, (((0,), (0,)), ((), ())), preferred_element_type=jnp.float32
    )
    projection = lax.psum_scatter(partial_value, "pix", scatter_dimension=0, tiled=True)
    basis_out = (own_basis * math.sqrt(total_rows)).reshape(1, 2 * share_pix, RANK)
    r_factor = lower_factor.T / math.sqrt(total_rows * ACT)
    return (basis_out, projection, r_factor)


def solution(mesh):
    return jax.shard_map(
        on_device,
        mesh=mesh,
        in_specs=(
            P("pix", None),
            P("act"),
            P("act", None),
            P("pix", None, "act"),
            P("pix"),
            P("pix"),
        ),
        out_specs=(P("pix", "act", None), P("pix", "act"), P()),
        check_vma=False,
    )
```

profile of v0, /device:TPU:2, one launch (start us, length us, event | category | flops | bytes accessed | tf_op | source)
XLA Modules:
  0.0 285.0 jit_solution(6364925790602597482)
XLA Ops:
  7.2 0.0 all-reduce.3.cloned.1.call-start
  7.9 0.7 fusion.16
  8.6 0.7 exponential_multiply_fusion
  10.0 0.7 fusion.9
  10.7 0.8 fusion.21
  11.4 0.7 multiply_divide_fusion
  12.1 9.1 %multiply_convert_fusion.1 = (bf16[512,1024]{1,0:T(8,128)(2,1)S(1)}, bf16[512,1024]{1,0:T(8,128)(2,1)S(1)}) fusion(f32[1024]{0:T(1024)S(1)} %bitcast.32, s32[1024]{0:T(1024)S(1)} %get-tuple-element.17, s32[512]{0:T(512)S(1)} %fusion.16, s32[1024]{0:T(1024)S(1)} %get-tuple-element.18, s32[512]{0:T(512)S(1)} %get-tuple-element.7, f32[]{:T(128)S(6)} %mul_shard_map.3, ...), kind=kLoop, calls=%fused_computation.2 | loop fusion | flops 8912896 | bytes 2125828 | tf_op jit(solution)/shard_map/convert_element_type | solution.py:33
  21.2 1.5 fusion.3
  22.8 0.0 all-reduce.5.cloned.1.call-start
  22.8 116.9 %all-reduce.3.cloned.1.call-done = f32[1024,128]{1,0:T(8,128)} async-done(((f32[1024,128]{1,0:T(8,128)}), f32[1024,128]{1,0:T(8,128)}) %all-reduce.3.cloned.1.call-update) | async-done | bytes 524304 | tf_op jit(solution)/shard_map/psum | solution.py:59
  139.7 2.9 %fusion.22 = f32[128,128]{0,1:T(8,128)} fusion(f32[1024,128]{1,0:T(8,128)} %all-reduce.3.cloned.1.call-done), kind=kOutput, calls=%fused_computation.58 | convolution fusion | flops 201326592 | bytes 589824 | tf_op jit(solution)/shard_map/dot_general | solution.py:37
  142.7 0.0 reduce-scatter.2.cloned.1.call-start
  142.7 72.8 %all-reduce.5.cloned.1.call-done = f32[128,128]{0,1:T(8,128)} async-done(((f32[128,128]{0,1:T(8,128)}), f32[128,128]{0,1:T(8,128)}) %all-reduce.5.cloned.1.call-update) | async-done | bytes 65552 | tf_op jit(solution)/shard_map/psum | solution.py:60
  215.5 0.9 copy.10
  216.4 0.9 fusion.7
  217.3 11.7 %cholesky.16 = f32[128,128]{1,0:T(8,128)S(1)} custom-call(f32[128,128]{1,0:T(8,128)S(1)} %fusion.7), custom_call_target="Cholesky" | custom-call | tf_op jit(solution)/shard_map/jit(cholesky)/cholesky | solution.py:61
  229.0 0.6 compare_reduce_fusion
  229.7 0.7 multiply_bitcast_fusion
  230.3 9.8 %custom-call.7 = f32[1,128,128]{1,2,0:T(8,128)S(1)} custom-call(f32[1,128,128]{2,1,0:T(8,128)S(1)} %get-tuple-element.11), custom_call_target="InvertDiagBlocksLowerTriangular" | custom-call | tf_op jit(solution)/shard_map/jit(_solve_triangular)/triangular_solve | solution.py:62
  240.1 0.6 fusion.5
  240.7 1.3 fusion.2
  242.0 0.7 copy.11
  242.7 0.6 maximum_multiply_fusion
  243.4 35.1 %reduce-scatter.2.cloned.1.call-done = f32[16,1024]{1,0:T(8,128)} async-done(((f32[128,1024]{1,0:T(8,128)}), f32[16,1024]{1,0:T(8,128)}) %reduce-scatter.2.cloned.1.call-update) | async-done | bytes 65552 | tf_op jit(solution)/shard_map/reduce_scatter | solution.py:71
  (9 shorter events, 0.1 us)
Async XLA Ops:
  7.2 14.1 %copy-start = (bf16[1024,128]{1,0:T(8,128)(2,1)S(1)}, bf16[1024,128]{1,0:T(8,128)(2,1)}, u32[]{:S(2)}) copy-start(bf16[1024,128]{1,0:T(8,128)(2,1)} %param.8) | copy-start | bytes 786436
  7.2 132.6 %all-reduce.3.cloned.1.call-start = ((), (), s32[]{:S(2)}) async-start(), calls=%async_computation.1 | async-start | bytes 1048576 | tf_op jit(solution)/shard_map/psum | solution.py:59
  22.8 192.7 %all-reduce.5.cloned.1.call-start = ((), (), s32[]{:S(2)}) async-start(), calls=%async_computation.2 | async-start | bytes 131072 | tf_op jit(solution)/shard_map/psum | solution.py:60
  139.7 100.4 %copy-start.1 = (f32[1024,128]{1,0:T(8,128)S(1)}, f32[1024,128]{1,0:T(8,128)}, u32[]{:S(2)}) copy-start(f32[1024,128]{1,0:T(8,128)} %all-reduce.3.cloned.1.call-done) | copy-start | bytes 1572868
  142.7 135.8 %reduce-scatter.2.cloned.1.call-start = ((), (), s32[]{:S(2)}) async-start(), calls=%async_computation.3 | async-start | bytes 589824 | tf_op jit(solution)/shard_map/reduce_scatter | solution.py:71
Sparse Core Ops, SparseCore 0:
  22.9 116.8 all-reduce.2
  142.8 72.6 all-reduce.4
  242.1 36.2 reduce-scatter.1
where the time goes:
time: 285 us
  waiting for transfers between devices  225 us (79%)
  other arithmetic  36.2 us (13%)
  between operations  15.2 us (5%)
  matrix products  6.22 us (2%)
    psum x1, waiting for transfers between devices, on_device(): sketch = lax.psum(partial_sketch, 'act')  117 us
    psum x1, waiting for transfers between devices, on_device(): gram_matrix = lax.psum(gram_of(sketch), 'pix')  72.8 us
    reduce_scatter x1, waiting for transfers between devices, on_device(): lax.psum_scatter(partial_value, 'pix', scatter_dimension=0, tiled=True)  35.1 us
    another operation x3, other arithmetic, on_device(): lower_factor = jnp.linalg.cholesky(gram_matrix)  12.4 us
    another operation x1, other arithmetic, on_device(): jax.scipy.linalg.solve_triangular(lower_factor, sketch.T, lower=True)  9.81 us
    convert_element_type x1, other arithmetic, jacobian_planes(): return (real_part.astype(jnp.bfloat16), imag_part.astype(jnp.bfloat16))  9.06 us
  transfers between devices with their start and end apart: 3, of which 3 were waited for; matrix products, arithmetic and copies ran while one was open for 0% of the time, Pallas kernels for 0%

commit v1 on v0

--- a/solution.py
+++ b/solution.py
@@ -56,7 +56,9 @@
     )
     jac = jnp.concatenate([real_rows, imag_rows], axis=0)
     partial_sketch = jnp.dot(jac, omega, preferred_element_type=jnp.float32)
-    sketch = lax.psum(partial_sketch, "act")
+    sketch = partial_sketch
+    for hop in (1, 2, 4, 8, 16):
+        sketch = sketch + lax.ppermute(sketch, "act", [(dev, dev ^ hop) for dev in range(32)])
     gram_matrix = lax.psum(gram_of(sketch), "pix")
     lower_factor = jnp.linalg.cholesky(gram_matrix)
     basis = jax.scipy.linalg.solve_triangular(lower_factor, sketch.T, lower=True).T

time: 285 us -> 226 us (0.79)
  waiting for transfers between devices: 225 us -> 157 us
  starting transfers between devices: 0.12 us -> 9.34 us
    psum x1 -> x0, waiting for transfers between devices: 117 us -> none  [on_device(): sketch = lax.psum(partial_sketch, 'act')]
    ppermute x0 -> x5, waiting for transfers between devices: none -> 47.8 us  [on_device(): lax.ppermute(sketch, 'act', [(dev, dev ^ hop) for dev in range(32)])]
    ppermute x0 -> x5, starting transfers between devices: none -> 9.08 us  [on_device(): lax.ppermute(sketch, 'act', [(dev, dev ^ hop) for dev in range(32)])]
  transfers between devices with their start and end apart: 3 -> 7, of which waited for: 3 -> 7; matrix products, arithmetic and copies ran while one was open for 0% -> 1% of each run, Pallas kernels for 0% -> 0%
where the time goes in v1:
time: 226 us; the launch traced here: 225 us
  waiting for transfers between devices  157 us (69%)
  other arithmetic  36.5 us (16%)
  between operations  15.5 us (7%)
  starting transfers between devices  9.34 us (4%)
  matrix products  4.17 us (2%)
  local copies, waits for them, and re-layouts  2.45 us (1%)
    psum x1, waiting for transfers between devices, on_device(): gram_matrix = lax.psum(gram_of(sketch), 'pix')  74.4 us
    ppermute x5, waiting for transfers between devices, on_device(): lax.ppermute(sketch, 'act', [(dev, dev ^ hop) for dev in range(32)])  47.8 us
    reduce_scatter x1, waiting for transfers between devices, on_device(): lax.psum_scatter(partial_value, 'pix', scatter_dimension=0, tiled=True)  35 us
    another operation x3, other arithmetic, on_device(): lower_factor = jnp.linalg.cholesky(gram_matrix)  12.4 us
    another operation x1, other arithmetic, on_device(): jax.scipy.linalg.solve_triangular(lower_factor, sketch.T, lower=True)  9.81 us
    ppermute x5, starting transfers between devices, on_device(): lax.ppermute(sketch, 'act', [(dev, dev ^ hop) for dev in range(32)])  9.08 us
    convert_element_type x1, other arithmetic, jacobian_planes(): return (real_part.astype(jnp.bfloat16), imag_part.astype(jnp.bfloat16))  9.06 us
  transfers between devices with their start and end apart: 7, of which 7 were waited for; matrix products, arithmetic and copies ran while one was open for 1% of the time, Pallas kernels for 0%

profile of v1, /device:TPU:2, one launch (start us, length us, event | category | flops | bytes accessed | tf_op | source)
XLA Modules:
  0.0 225.2 jit_solution(9387717641315229778)
XLA Ops:
  8.6 0.7 exponential_multiply_fusion
  10.0 0.7 fusion.9
  10.7 0.8 fusion.21
  11.4 0.7 multiply_divide_fusion
  12.1 9.1 %multiply_convert_fusion.1 = (bf16[512,1024]{1,0:T(8,128)(2,1)S(1)}, bf16[512,1024]{1,0:T(8,128)(2,1)S(1)}) fusion(f32[1024]{0:T(1024)S(1)} %bitcast.32, s32[1024]{0:T(1024)S(1)} %get-tuple-element.17, s32[512]{0:T(512)S(1)} %fusion.16, s32[1024]{0:T(1024)S(1)} %get-tuple-element.18, s32[512]{0:T(512)S(1)} %get-tuple-element.7, f32[]{:T(128)S(6)} %mul_shard_map.3, ...), kind=kLoop, calls=%fused_computation.2 | loop fusion | flops 8912896 | bytes 2125828 | tf_op jit(solution)/shard_map/convert_element_type | solution.py:33
  21.2 0.7 fusion.3
  22.0 1.9 collective-permute-done
  24.0 1.7 collective-permute-start.1
  25.7 12.4 %collective-permute-done.1 = f32[1024,128]{1,0:T(8,128)S(1)} collective-permute-done((f32[1024,128]{1,0:T(8,128)S(1)}, f32[1024,128]{1,0:T(8,128)S(1)}, u32[]{:S(2)}, u32[]{:S(2)}) %collective-permute-start.1) | collective-permute-done | bytes 524320 | tf_op jit(solution)/shard_map/ppermute | solution.py:61
  38.1 3.3 %collective-permute-start.2 = (f32[1024,128]{1,0:T(8,128)S(1)}, f32[1024,128]{1,0:T(8,128)S(1)}, u32[]{:S(2)}, u32[]{:S(2)}) collective-permute-start(f32[1024,128]{1,0:T(8,128)S(1)} %add.125), channel_id=1, source_target_pairs={{0,32},{8,40},{16,48},{24,56},{32,0},{40,8},{48,16},{56,24},{64,96... | collective-permute-start | bytes 1572872 | tf_op jit(solution)/shard_map/ppermute | solution.py:61
  41.4 11.4 %collective-permute-done.2 = f32[1024,128]{1,0:T(8,128)S(1)} collective-permute-done((f32[1024,128]{1,0:T(8,128)S(1)}, f32[1024,128]{1,0:T(8,128)S(1)}, u32[]{:S(2)}, u32[]{:S(2)}) %collective-permute-start.2) | collective-permute-done | bytes 524320 | tf_op jit(solution)/shard_map/ppermute | solution.py:61
  52.9 2.3 %collective-permute-start.3 = (f32[1024,128]{1,0:T(8,128)S(1)}, f32[1024,128]{1,0:T(8,128)S(1)}, u32[]{:S(2)}, u32[]{:S(2)}) collective-permute-start(f32[1024,128]{1,0:T(8,128)S(1)} %add.126), channel_id=1, source_target_pairs={{0,64},{8,72},{16,80},{24,88},{32,96},{40,104},{48,112},{56,120},{... | collective-permute-start | bytes 1572872 | tf_op jit(solution)/shard_map/ppermute | solution.py:61
  55.2 10.5 %collective-permute-done.3 = f32[1024,128]{1,0:T(8,128)S(1)} collective-permute-done((f32[1024,128]{1,0:T(8,128)S(1)}, f32[1024,128]{1,0:T(8,128)S(1)}, u32[]{:S(2)}, u32[]{:S(2)}) %collective-permute-start.3) | collective-permute-done | bytes 524320 | tf_op jit(solution)/shard_map/ppermute | solution.py:61
  65.8 1.7 collective-permute-start.4
  67.5 11.6 %collective-permute-done.4 = f32[1024,128]{1,0:T(8,128)S(1)} collective-permute-done((f32[1024,128]{1,0:T(8,128)S(1)}, f32[1024,128]{1,0:T(8,128)S(1)}, u32[]{:S(2)}, u32[]{:S(2)}) %collective-permute-start.4) | collective-permute-done | bytes 524320 | tf_op jit(solution)/shard_map/ppermute | solution.py:61
  79.1 1.6 fusion.22
  81.0 74.4 %all-reduce.2.cloned.1.call-done = f32[128,128]{0,1:T(8,128)} async-done(((f32[128,128]{0,1:T(8,128)}), f32[128,128]{0,1:T(8,128)}) %all-reduce.2.cloned.1.call-update) | async-done | bytes 65552 | tf_op jit(solution)/shard_map/psum | solution.py:62
  155.4 0.9 copy.10
  156.4 0.9 fusion.7
  157.2 11.7 %cholesky.16 = f32[128,128]{1,0:T(8,128)S(1)} custom-call(f32[128,128]{1,0:T(8,128)S(1)} %fusion.7), custom_call_target="Cholesky" | custom-call | tf_op jit(solution)/shard_map/jit(cholesky)/cholesky | solution.py:63
  170.3 9.8 %custom-call.7 = f32[1,128,128]{1,2,0:T(8,128)S(1)} custom-call(f32[1,128,128]{2,1,0:T(8,128)S(1)} %get-tuple-element.11), custom_call_target="InvertDiagBlocksLowerTriangular" | custom-call | tf_op jit(solution)/shard_map/jit(_solve_triangular)/triangular_solve | solution.py:64
  180.7 1.3 fusion.2
  182.0 0.7 copy.11
  183.3 35.0 %reduce-scatter.2.cloned.1.call-done = f32[16,1024]{1,0:T(8,128)} async-done(((f32[128,1024]{1,0:T(8,128)}), f32[16,1024]{1,0:T(8,128)}) %reduce-scatter.2.cloned.1.call-update) | async-done | bytes 65552 | tf_op jit(solution)/shard_map/reduce_scatter | solution.py:73
  (19 shorter events, 3.9 us)
Async XLA Ops:
  7.2 14.1 %copy-start = (bf16[1024,128]{1,0:T(8,128)(2,1)S(1)}, bf16[1024,128]{1,0:T(8,128)(2,1)}, u32[]{:S(2)}) copy-start(bf16[1024,128]{1,0:T(8,128)(2,1)} %param.8) | copy-start | bytes 786436
  7.2 148.3 %all-reduce.2.cloned.1.call-start = ((), (), s32[]{:S(2)}) async-start(), calls=%async_computation.1 | async-start | bytes 131072 | tf_op jit(solution)/shard_map/psum | solution.py:62
  21.9 2.0 collective-permute-start
  24.0 14.1 %collective-permute-start.1 = (f32[1024,128]{1,0:T(8,128)S(1)}, f32[1024,128]{1,0:T(8,128)S(1)}, u32[]{:S(2)}, u32[]{:S(2)}) collective-permute-start(f32[1024,128]{1,0:T(8,128)S(1)} %add.124), channel_id=1, source_target_pairs={{0,16},{8,24},{16,0},{24,8},{32,48},{40,56},{48,32},{56,40},{64,80... | collective-permute-start | bytes 1572872 | tf_op jit(solution)/shard_map/ppermute | solution.py:61
  38.1 14.7 %collective-permute-start.2 = (f32[1024,128]{1,0:T(8,128)S(1)}, f32[1024,128]{1,0:T(8,128)S(1)}, u32[]{:S(2)}, u32[]{:S(2)}) collective-permute-start(f32[1024,128]{1,0:T(8,128)S(1)} %add.125), channel_id=1, source_target_pairs={{0,32},{8,40},{16,48},{24,56},{32,0},{40,8},{48,16},{56,24},{64,96... | collective-permute-start | bytes 1572872 | tf_op jit(solution)/shard_map/ppermute | solution.py:61
  52.9 12.8 %collective-permute-start.3 = (f32[1024,128]{1,0:T(8,128)S(1)}, f32[1024,128]{1,0:T(8,128)S(1)}, u32[]{:S(2)}, u32[]{:S(2)}) collective-permute-start(f32[1024,128]{1,0:T(8,128)S(1)} %add.126), channel_id=1, source_target_pairs={{0,64},{8,72},{16,80},{24,88},{32,96},{40,104},{48,112},{56,120},{... | collective-permute-start | bytes 1572872 | tf_op jit(solution)/shard_map/ppermute | solution.py:61
  65.8 13.3 %collective-permute-start.4 = (f32[1024,128]{1,0:T(8,128)S(1)}, f32[1024,128]{1,0:T(8,128)S(1)}, u32[]{:S(2)}, u32[]{:S(2)}) collective-permute-start(f32[1024,128]{1,0:T(8,128)S(1)} %add.127), channel_id=1, source_target_pairs={{0,128},{8,136},{16,144},{24,152},{32,160},{40,168},{48,176},{56,1... | collective-permute-start | bytes 1572872 | tf_op jit(solution)/shard_map/ppermute | solution.py:61
  80.8 137.6 %reduce-scatter.2.cloned.1.call-start = ((), (), s32[]{:S(2)}) async-start(), calls=%async_computation.2 | async-start | bytes 589824 | tf_op jit(solution)/shard_map/reduce_scatter | solution.py:73
Sparse Core Ops, SparseCore 0:
  80.9 74.4 all-reduce.1
  182.1 36.2 reduce-scatter.1
